TPU v7x, 32 devices: a whole 2x2x4 slice. The times are simulated.
32 devices in a mesh: seq: 8 (over z, y), fsdp: 4 (over x, core).
Axes of the slice: x: 2, y: 2, z: 4, core: 2. Of those that a mesh axis runs over, the one named last changes fastest.
Arguments:
- tokens: bfloat16 [2048, 2048], P('seq', 'fsdp'), may hold values from -6 to 6
- deal_order: int32 [8, 8], replicated, may hold values from 0 to 7, each once within a row
- lengths: int32 [4], replicated, may hold values from 1 to 1024, 2048 in all
- x_weight: bfloat16 [2048, 1536], P(None, 'fsdp'), may hold values from -0.0390625 to 0.0390625
- z_weight: bfloat16 [2048, 1536], P(None, 'fsdp'), may hold values from -0.125 to 0.125
- shared_weight: bfloat16 [2048, 512], P('fsdp'), may hold values from -0.0390625 to 0.0390625
- step_weight: bfloat16 [2048, 24], P(None, 'fsdp'), may hold values from -0.125 to 0.125
- conv_heads: float32 [4, 1536], P(None, 'fsdp'), may hold values from -3 to 3
- conv_shared: float32 [4, 512], replicated, may hold values from -3 to 3
- step_bias: float32 [24], P('fsdp'), as said below
- decay_log: float32 [24], P('fsdp'), may hold values from -7.1 to -2.8, as said below
- skip_gain: float32 [24], P('fsdp'), may hold values from 0.5 to 1.5
Outputs:
- mixed: bfloat16 [2048, 1536], P('seq', 'fsdp')
Inputs may be any that keep to these rules, and one draw needn't show every extreme that they name: `deal_order`: each row is a permutation of 0 to 7. The lengths sum to 2048. `decay_log`: one value a head. `step_bias`: one value a head.
All inputs are finite; a program needn't handle non-finite values.
Results may differ from a plain program's by a relative error of at most 0.0095.
Values may be sent and summed in bfloat16 or wider, within the bound.
No kernel may reach another device: no remote copies, remote signals or barrier semaphores. Data moves between devices by JAX's collectives and lax.ppermute only.
A program may use at most 128 MiB of HBM per device.

v0:
```python
import jax
import jax.numpy as jnp
from jax import lax
from jax.sharding import PartitionSpec as P

precise = lax.Precision.HIGHEST


def shifted(array, axis, by):
    count = lax.axis_size(axis)
    pairs = [(i, i + by) for i in range(count) if 0 <= i + by < count]
    return lax.ppermute(array, axis, pairs)


def combine_packed(earlier, later):
    rows = later.shape[1] - 1
    d_e, d_l = (earlier[:, rows:, :], later[:, rows:, :])
    return jnp.concatenate([d_l * earlier[:, :rows, :] + later[:, :rows, :], d_e * d_l], axis=1)


def received(packed, axis, by):
    place = lax.axis_index(axis)
    got = shifted(packed, axis, by)
    rows = packed.shape[1] - 1
    missing = (place < by).astype(packed.dtype)
    return got.at[:, rows:, :].add(missing)


def exclusive_scan(packed, axis):
    count = lax.axis_size(axis)
    if count == 1:
        return received(packed, axis, 1)
    held = received(packed, axis, 1)
    if count > 2:
        held = combine_packed(received(packed, axis, 2), held)
    cover = 2
    while cover < count - 1:
        held = combine_packed(received(held, axis, cover), held)
        cover *= 2
    return held


def segment_of(positions, lengths):
    prompt_ends = jnp.cumsum(lengths)
    counted = (positions[:, None] >= prompt_ends[None, :]).astype(jnp.int32)
    return jnp.sum(counted, axis=1)


def causal_conv(extended, segment_ids, weights, conv_width):
    out_rows = extended.shape[0] - conv_width + 1
    target = segment_ids[conv_width - 1 :]
    running = jnp.zeros((out_rows, extended.shape[1]), jnp.float32)
    for tap_index in range(conv_width):
        matched = (segment_ids[tap_index : tap_index + out_rows] == target).astype(jnp.float32)
        running = (
            running
            + weights[tap_index][None, :]
            * extended[tap_index : tap_index + out_rows]
            * matched[:, None]
        )
    return running


def local_terms(x_heads, b_rows, c_rows, step_size, decay_log, segment_ids, seg_before):
    log_decay = -jnp.exp(decay_log)[None, :] * step_size
    cum_decay = jnp.cumsum(log_decay, axis=0)
    positions_in = jnp.arange(x_heads.shape[0], dtype=jnp.int32)
    same_prompt = (segment_ids[:, None] == segment_ids[None, :]) & (
        positions_in[:, None] >= positions_in[None, :]
    )
    decay_gap = cum_decay.T[:, :, None] - cum_decay.T[:, None, :]
    decay_matrix = jnp.exp(jnp.where(same_prompt[None], decay_gap, -jnp.inf))
    scores = jnp.dot(c_rows, b_rows.T, precision=precise)
    x_step = x_heads * step_size[:, :, None]
    intra = jnp.einsum("hts,shp->thp", scores[None] * decay_matrix, x_step, precision=precise)
    to_end = jnp.exp(
        jnp.where(
            (segment_ids == segment_ids[-1])[:, None], cum_decay[-1][None, :] - cum_decay, -jnp.inf
        )
    )
    state_out = jnp.einsum("shp,sn->hpn", x_step * to_end[:, :, None], b_rows, precision=precise)
    carried = segment_ids == seg_before
    carry_in = jnp.exp(jnp.where(carried[:, None], cum_decay, -jnp.inf))
    block_decay = jnp.where(carried[-1], jnp.exp(cum_decay[-1]), 0.0)
    return (intra, state_out, carry_in, block_decay)


def per_device(
    tokens,
    deal_order,
    lengths,
    x_weight,
    z_weight,
    shared_weight,
    step_weight,
    conv_heads,
    conv_shared,
    step_bias,
    decay_log,
    skip_gain,
):
    seq_count = lax.axis_size("seq")
    own_index = lax.axis_index("seq")
    tok_dev = tokens.shape[0]
    piece_rows = tok_dev // seq_count
    slot_rows = tokens.reshape(seq_count, piece_rows, tokens.shape[1])
    arrived = lax.all_to_all(slot_rows, "seq", split_axis=0, concat_axis=0, tiled=True)
    dealt_row = lax.dynamic_slice_in_dim(deal_order, own_index, 1, 0)[0]
    inverse = jnp.argsort(dealt_row)
    stream_block = jnp.take(arrived, inverse, axis=0).reshape(tok_dev, tokens.shape[1])
    inner_dev = x_weight.shape[1]
    heads_dev = step_weight.shape[1]
    head_dim = inner_dev // heads_dev
    state_dim = shared_weight.shape[1] // 2
    w_full = lax.all_gather(shared_weight, "fsdp", axis=0, tiled=True)
    weight_list = (x_weight, z_weight, step_weight, w_full)
    feature_part = lax.all_gather(stream_block, "fsdp", axis=1, tiled=True)
    x_acc, z_acc, step_acc, bc_acc = tuple(
        (
            jnp.dot(feature_part, weight, preferred_element_type=jnp.float32)
            for weight in weight_list
        )
    )
    x_raw = x_acc.astype(jnp.bfloat16)
    z_raw = z_acc.astype(jnp.bfloat16)
    bc_raw = bc_acc.astype(jnp.bfloat16)
    step_size = jax.nn.softplus(step_acc + step_bias[None, :])
    mixed_in = jnp.concatenate([x_raw, bc_raw], axis=1)
    conv_width = conv_heads.shape[0]
    prior_rows = shifted(mixed_in[tok_dev - conv_width + 1 :], "seq", 1)
    first_pos = own_index * tok_dev
    positions = first_pos - (conv_width - 1) + jnp.arange(tok_dev + conv_width - 1, dtype=jnp.int32)
    seg_ext = segment_of(positions, lengths)
    extended = jnp.concatenate([prior_rows, mixed_in], axis=0).astype(jnp.float32)
    activated = jax.nn.silu(
        causal_conv(
            extended, seg_ext, jnp.concatenate([conv_heads, conv_shared], axis=1), conv_width
        )
    )
    segment_ids = seg_ext[conv_width - 1 :]
    seg_before = jnp.where(own_index == 0, -1, seg_ext[conv_width - 2])
    x_heads = activated[:, :inner_dev].reshape(tok_dev, heads_dev, head_dim)
    b_rows = activated[:, inner_dev : inner_dev + state_dim]
    c_rows = activated[:, inner_dev + state_dim :]
    intra, state_out, carry_in, block_decay = local_terms(
        x_heads, b_rows, c_rows, step_size, decay_log, segment_ids, seg_before
    )
    packed = jnp.concatenate(
        [state_out, jnp.broadcast_to(block_decay[:, None, None], (heads_dev, 1, state_dim))], axis=1
    )
    state_in = exclusive_scan(packed, "seq")[:, :head_dim, :]
    incoming = jnp.einsum("tn,hpn->thp", c_rows, state_in, precision=precise)
    y_block = intra + carry_in[:, :, None] * incoming + skip_gain[None, :, None] * x_heads
    gated = (y_block.reshape(tok_dev, inner_dev) * jax.nn.silu(z_raw.astype(jnp.float32))).astype(
        jnp.bfloat16
    )
    ordered = gated.reshape(seq_count, piece_rows, inner_dev)
    outgoing = jnp.take(ordered, dealt_row, axis=0)
    returned = lax.all_to_all(outgoing, "seq", split_axis=0, concat_axis=0, tiled=True)
    return returned.reshape(tok_dev, inner_dev)


def solution(mesh):
    return jax.shard_map(
        per_device,
        mesh=mesh,
        in_specs=(
            P("seq", "fsdp"),
            P(),
            P(),
            P(None, "fsdp"),
            P(None, "fsdp"),
            P("fsdp", None),
            P(None, "fsdp"),
            P(None, "fsdp"),
            P(),
            P("fsdp"),
            P("fsdp"),
            P("fsdp"),
        ),
        out_specs=P("seq", "fsdp"),
        check_vma=False,
    )
```

profile of v0, /device:TPU:0, one launch (start us, length us, event | category | flops | bytes accessed | tf_op | source)
XLA Modules:
  0.0 161.2 jit_solution(1924981026122222076)
XLA Ops:
  6.6 7.4 %all-to-all-start = ((bf16[8,32,512]{2,1,0:T(8,128)(2,1)}), bf16[8,32,512]{2,1,0:T(8,128)(2,1)S(1)}, u32[]{:S(2)}, u32[]{:S(2)}) async-start(bf16[8,32,512]{2,1,0:T(8,128)(2,1)} %bitcast.85), calls=%async_computation | async-start | bytes 524288 | tf_op jit(solution)/shard_map/all_to_all | solution.py:107
  14.0 1.3 compare_and_fusion.1
  15.3 1.0 sort.17
  16.3 0.1 broadcast_in_dim.93
  16.4 0.1 broadcast_in_dim.94
  16.5 6.4 %all-to-all-done = bf16[8,32,512]{2,1,0:T(8,128)(2,1)S(1)} async-done(((bf16[8,32,512]{2,1,0:T(8,128)(2,1)}), bf16[8,32,512]{2,1,0:T(8,128)(2,1)S(1)}, u32[]{:S(2)}, u32[]{:S(2)}) %all-to-all-start) | async-done | bytes 262176 | tf_op jit(solution)/shard_map/all_to_all | solution.py:107
  22.9 0.6 gather_fusion
  23.5 0.8 bitcast_select_fusion
  24.3 0.0 all-gather.5.cloned.1.call-start
  24.4 0.7 all-gather.5.cloned.1.call-update
  25.1 0.2 reduce-window.18
  25.3 0.1 convert_reduce_fusion
  25.4 0.6 fusion.53
  26.5 1.3 broadcast_compare_fusion
  27.9 0.7 slice.199
  28.5 0.6 slice_reduce_fusion.4
  29.2 11.1 %all-gather.3.cloned.1.call-done = bf16[256,2048]{1,0:T(8,128)(2,1)} async-done(((bf16[256,512]{1,0:T(8,128)(2,1)}), bf16[256,2048]{1,0:T(8,128)(2,1)}) %all-gather.3.cloned.1.call-update) | async-done | bytes 1048592 | tf_op jit(solution)/shard_map/all_gather | solution.py:117
  40.2 1.6 %fusion.41 = (f32[6,256]{1,0:T(8,128)S(1)}, f32[256,6]{0,1:T(8,128)S(1)}) fusion(f32[6]{0:T(128)S(1)} %exponential_negate_fusion, f32[6]{0:T(128)S(1)} %copy-done.19, bf16[256,2048]{1,0:T(8,128)(2,1)} %all-gather.3.cloned.1.call-done, bf16[2048,6]{0,1:T(8,128)(2,1)S(1)} %copy-done.4), kind=kOutput, calls=%fused_computation.64 | convolution fusion | flops 6303744 | bytes 1085488 | tf_op jit(solution)/shard_map/dot_general | solution.py:120
  41.9 1.8 %reduce-window.19 = f32[6,2,128]{2,1,0:T(2,128)S(1)} reduce-window(f32[6,2,128]{2,1,0:T(2,128)S(1)} %reshape.288, f32[]{:T(128)} %constant.149.clone.1), window={size=1x1x128 pad=0_0x0_0x127_0}, to_apply=%region_3.4 | reduce-window | flops 195072 | bytes 12292 | tf_op jit(solution)/shard_map/reduce-window.1
  43.7 0.1 slice.222
  43.8 0.1 copy.40
  43.9 0.1 copy.41
  44.0 0.1 add_bitcast_fusion
  44.1 0.2 slice_reduce_fusion
  44.3 0.4 copy-done.7
  44.7 0.7 select_exponential_fusion.1
  45.4 1.9 %convolution_convert_fusion.2 = bf16[256,384]{1,0:T(8,128)(2,1)S(1)} fusion(bf16[256,2048]{1,0:T(8,128)(2,1)} %all-gather.3.cloned.1.call-done, bf16[2048,384]{1,0:T(8,128)(2,1)S(1)} %copy-done), kind=kOutput, calls=%fused_computation.14 | convolution fusion | flops 402751488 | bytes 2818048 | tf_op jit(solution)/shard_map/dot_general | solution.py:120
  47.3 17.1 %all-gather.5.cloned.1.call-done = bf16[2048,512]{1,0:T(8,128)(2,1)} async-done(((bf16[512,512]{1,0:T(8,128)(2,1)}), bf16[2048,512]{1,0:T(8,128)(2,1)}) %all-gather.5.cloned.1.call-update) | async-done | bytes 2097168 | tf_op jit(solution)/shard_map/all_gather | solution.py:115
  64.4 2.3 %convolution_convert_fusion = bf16[256,512]{1,0:T(8,128)(2,1)S(1)} fusion(bf16[256,2048]{1,0:T(8,128)(2,1)S(1)} %copy-done.1, bf16[2048,512]{1,0:T(8,128)(2,1)} %all-gather.5.cloned.1.call-done), kind=kOutput, calls=%fused_computation.8 | convolution fusion | flops 537001984 | bytes 3407872 | tf_op jit(solution)/shard_map/dot_general | solution.py:120
  66.8 3.4 %collective-permute-start = (bf16[3,896]{1,0:T(4,128)(2,1)S(1)}, bf16[3,896]{1,0:T(4,128)(2,1)S(1)}, u32[]{:S(2)}, u32[]{:S(2)}) collective-permute-start(bf16[3,896]{1,0:T(4,128)(2,1)S(1)} %pad_maximum_fusion.3), channel_id=1, source_target_pairs={{0,4},{4,8},{8,12},{12,16},{16,20},{20,24},{24,28},{1,5},{5,9},{9,... | collective-permute-start | bytes 16136 | tf_op jit(solution)/shard_map/ppermute | solution.py:12
  70.2 1.2 broadcast_select_fusion.1
  71.4 0.1 collective-permute-done
  71.5 0.1 maximum_convert_fusion
  71.7 0.7 divide_multiply_fusion
  72.4 0.8 slice.219
  73.1 1.9 %copy.39 = f32[256,384]{0,1:T(8,128)} copy(f32[256,384]{1,0:T(8,128)} %slice.219) | data formatting | bytes 786432 | tf_op jit(solution)/shard_map/slice | solution.py:142
  75.1 1.5 fusion.25
  76.5 0.7 broadcast_in_dim.104
  77.3 0.8 pad_maximum_fusion
  78.1 5.9 %collective-permute-start.2 = (f32[6,65,256]{2,1,0:T(8,128)}, f32[6,65,256]{2,1,0:T(8,128)}, u32[]{:S(2)}, u32[]{:S(2)}) collective-permute-start(f32[6,65,256]{2,1,0:T(8,128)} %pad_maximum_fusion), channel_id=1, source_target_pairs={{0,8},{4,12},{8,16},{12,20},{16,24},{20,28},{1,9},{5,13},{9,17},{1... | collective-permute-start | bytes 1198088 | tf_op jit(solution)/shard_map/ppermute | solution.py:12
  83.9 3.2 %collective-permute-start.1 = (f32[6,65,256]{2,1,0:T(8,128)}, f32[6,65,256]{2,1,0:T(8,128)}, u32[]{:S(2)}, u32[]{:S(2)}) collective-permute-start(f32[6,65,256]{2,1,0:T(8,128)} %pad_maximum_fusion), channel_id=1, source_target_pairs={{0,4},{4,8},{8,12},{12,16},{16,20},{20,24},{24,28},{1,5},{5,9},{9,... | collective-permute-start | bytes 1198088 | tf_op jit(solution)/shard_map/ppermute | solution.py:12
  87.2 0.7 slice.182
  87.8 0.8 fusion.49
  88.7 0.9 fusion.31
  89.5 2.6 %collective-permute-done.2 = f32[6,65,256]{2,1,0:T(8,128)} collective-permute-done((f32[6,65,256]{2,1,0:T(8,128)}, f32[6,65,256]{2,1,0:T(8,128)}, u32[]{:S(2)}, u32[]{:S(2)}) %collective-permute-start.2) | collective-permute-done | bytes 399392 | tf_op jit(solution)/shard_map/ppermute | solution.py:12
  92.1 3.0 %collective-permute-done.1 = f32[6,65,256]{2,1,0:T(8,128)} collective-permute-done((f32[6,65,256]{2,1,0:T(8,128)}, f32[6,65,256]{2,1,0:T(8,128)}, u32[]{:S(2)}, u32[]{:S(2)}) %collective-permute-start.1) | collective-permute-done | bytes 399392 | tf_op jit(solution)/shard_map/ppermute | solution.py:12
  95.1 0.8 fusion.47
  96.0 1.2 slice_add_fusion
  97.2 10.9 %collective-permute-start.3 = (f32[6,65,256]{2,1,0:T(8,128)S(1)}, f32[6,65,256]{2,1,0:T(8,128)S(1)}, u32[]{:S(2)}, u32[]{:S(2)}) collective-permute-start(f32[6,65,256]{2,1,0:T(8,128)S(1)} %pad_maximum_fusion.1), channel_id=1, source_target_pairs={{0,8},{4,12},{8,16},{12,20},{16,24},{20,28},{1,9},{5,13},{9,17},{1... | collective-permute-start | bytes 1198088 | tf_op jit(solution)/shard_map/ppermute | solution.py:12
  108.1 0.6 pad_clamp_fusion
  108.7 1.4 fusion.10
  110.2 5.7 %collective-permute-done.3 = f32[6,65,256]{2,1,0:T(8,128)S(1)} collective-permute-done((f32[6,65,256]{2,1,0:T(8,128)S(1)}, f32[6,65,256]{2,1,0:T(8,128)S(1)}, u32[]{:S(2)}, u32[]{:S(2)}) %collective-permute-start.3) | collective-permute-done | bytes 399392 | tf_op jit(solution)/shard_map/ppermute | solution.py:12
  115.8 0.1 fusion.24
  116.0 5.3 %collective-permute-start.4 = (f32[6,65,256]{2,1,0:T(8,128)S(1)}, f32[6,65,256]{2,1,0:T(8,128)S(1)}, u32[]{:S(2)}, u32[]{:S(2)}) collective-permute-start(f32[6,65,256]{2,1,0:T(8,128)S(1)} %pad_maximum_fusion.2), channel_id=1, source_target_pairs={{0,16},{4,20},{8,24},{12,28},{1,17},{5,21},{9,25},{13,29},{2,18},{... | collective-permute-start | bytes 1198088 | tf_op jit(solution)/shard_map/ppermute | solution.py:12
  121.3 0.4 fusion.33
  121.7 1.9 %fusion.5 = f32[256,6,64]{0,2,1:T(8,128)S(1)} fusion(f32[6,256]{1,0:T(8,128)S(1)} %bitcast.90, f32[256,256]{1,0:T(8,128)S(1)} %fusion.33, pred[256,256]{1,0:T(8,128)(4,1)S(1)} %fusion.31, f32[256,6,64]{0,2,1:T(8,128)S(1)} %bitcast.80, f32[256,6]{0,1:T(8,128)S(1)} %get-tuple-element.76), kind=kOutput, calls=%fused_computation.7 | convolution fusion | flops 303267840 | bytes 1126400 | tf_op jit(solution)/shard_map/hts,shp->thp/dot_general | solution.py:75
  123.6 4.5 %collective-permute-done.4 = f32[6,65,256]{2,1,0:T(8,128)S(1)} collective-permute-done((f32[6,65,256]{2,1,0:T(8,128)S(1)}, f32[6,65,256]{2,1,0:T(8,128)S(1)}, u32[]{:S(2)}, u32[]{:S(2)}) %collective-permute-start.4) | collective-permute-done | bytes 399392 | tf_op jit(solution)/shard_map/ppermute | solution.py:12
  128.1 0.5 fusion.9
  128.7 0.2 copy.42
  128.8 1.1 multiply_convert_fusion
  129.9 0.7 gather_fusion.1
  130.7 0.1 broadcast_select_fusion
  130.8 22.9 %all_to_all.10 = bf16[8,32,384]{2,1,0:T(8,128)(2,1)S(1)} all-to-all(bf16[8,32,384]{2,1,0:T(8,128)(2,1)S(1)} %broadcast_select_fusion), channel_id=1, replica_groups=mesh['seq'=8,'fsdp'=4] {'seq'}, dimensions={0} | all-to-all | bytes 393216 | tf_op jit(solution)/shard_map/all_to_all | solution.py:159
  153.7 0.7 copy.63
  (66 shorter events, 0.3 us)
Async XLA Ops:
  6.5 38.8 %copy-start = (bf16[2048,384]{1,0:T(8,128)(2,1)S(1)}, bf16[2048,384]{1,0:T(8,128)(2,1)}, u32[]{:S(2)}) copy-start(bf16[2048,384]{1,0:T(8,128)(2,1)} %param.23) | copy-start | bytes 4718596
  6.5 18.5 %copy-start.21 = (s32[4]{0:T(128)S(1)}, s32[4]{0:T(128)}, u32[]{:S(2)}) copy-start(s32[4]{0:T(128)} %param.22) | copy-start | bytes 52
  6.5 22.0 %copy-start.14 = (f32[4,384]{1,0:T(4,128)S(1)}, f32[4,384]{1,0:T(4,128)}, u32[]{:S(2)}) copy-start(f32[4,384]{1,0:T(4,128)} %param.27) | copy-start | bytes 18436
  6.5 22.0 %copy-start.13 = (f32[4,512]{1,0:T(4,128)S(1)}, f32[4,512]{1,0:T(4,128)}, u32[]{:S(2)}) copy-start(f32[4,512]{1,0:T(4,128)} %param.28) | copy-start | bytes 24580
  6.5 22.6 %copy-start.22 = (f32[6]{0:T(128)S(1)}, f32[6]{0:T(128)}, u32[]{:S(2)}) copy-start(f32[6]{0:T(128)} %param.30) | copy-start | bytes 76
  6.5 33.7 %copy-start.19 = (f32[6]{0:T(128)S(1)}, f32[6]{0:T(128)}, u32[]{:S(2)}) copy-start(f32[6]{0:T(128)} %param.29) | copy-start | bytes 76
  6.6 33.7 %copy-start.4 = (bf16[2048,6]{0,1:T(8,128)(2,1)S(1)}, bf16[2048,6]{0,1:T(8,128)(2,1)}, u32[]{:S(2)}) copy-start(bf16[2048,6]{0,1:T(8,128)(2,1)} %param.26) | copy-start | bytes 73732
  6.6 16.3 %all-to-all-start = ((bf16[8,32,512]{2,1,0:T(8,128)(2,1)}), bf16[8,32,512]{2,1,0:T(8,128)(2,1)S(1)}, u32[]{:S(2)}, u32[]{:S(2)}) async-start(bf16[8,32,512]{2,1,0:T(8,128)(2,1)} %bitcast.85), calls=%async_computation | async-start | bytes 524288 | tf_op jit(solution)/shard_map/all_to_all | solution.py:107
  14.0 26.2 %all-gather.3.cloned.1.call-start = ((), (), s32[]{:S(2)}) async-start(), calls=%async_computation.2 | async-start | bytes 1310720 | tf_op jit(solution)/shard_map/all_gather | solution.py:117
  24.3 40.1 %all-gather.5.cloned.1.call-start = ((), (), s32[]{:S(2)}) async-start(), calls=%async_computation.3 | async-start | bytes 2621440 | tf_op jit(solution)/shard_map/all_gather | solution.py:115
  25.4 14.9 %copy-start.5 = (s32[259]{0:T(512)}, s32[259]{0:T(512)S(1)}, u32[]{:S(2)}) copy-start(s32[259]{0:T(512)S(1)} %convert_reduce_fusion) | copy-start | bytes 3112
  41.9 22.5 %copy-start.1 = (bf16[256,2048]{1,0:T(8,128)(2,1)S(1)}, bf16[256,2048]{1,0:T(8,128)(2,1)}, u32[]{:S(2)}) copy-start(bf16[256,2048]{1,0:T(8,128)(2,1)} %all-gather.3.cloned.1.call-done) | copy-start | bytes 3145732
  44.1 0.6 copy-start.7
  66.7 4.9 %copy-start.9 = (f32[896]{0:T(1024)S(1)}, f32[896]{0:T(1024)}, u32[]{:S(2)}) copy-start(f32[896]{0:T(1024)} %get-tuple-element.55) | copy-start | bytes 10756
  66.7 4.9 %copy-start.10 = (f32[896]{0:T(1024)S(1)}, f32[896]{0:T(1024)}, u32[]{:S(2)}) copy-start(f32[896]{0:T(1024)} %get-tuple-element.56) | copy-start | bytes 10756
  66.7 4.9 %copy-start.11 = (f32[896]{0:T(1024)S(1)}, f32[896]{0:T(1024)}, u32[]{:S(2)}) copy-start(f32[896]{0:T(1024)} %get-tuple-element.57) | copy-start | bytes 10756
  66.7 4.9 %copy-start.12 = (f32[896]{0:T(1024)S(1)}, f32[896]{0:T(1024)}, u32[]{:S(2)}) copy-start(f32[896]{0:T(1024)} %get-tuple-element.58) | copy-start | bytes 10756
  66.7 4.9 %copy-start.15 = (f32[256]{0:T(256)S(1)}, f32[256]{0:T(256)}, u32[]{:S(2)}) copy-start(f32[256]{0:T(256)} %get-tuple-element.69) | copy-start | bytes 3076
  66.8 4.9 %copy-start.16 = (f32[256]{0:T(256)S(1)}, f32[256]{0:T(256)}, u32[]{:S(2)}) copy-start(f32[256]{0:T(256)} %get-tuple-element.70) | copy-start | bytes 3076
  66.8 4.9 %copy-start.17 = (f32[256]{0:T(256)S(1)}, f32[256]{0:T(256)}, u32[]{:S(2)}) copy-start(f32[256]{0:T(256)} %get-tuple-element.71) | copy-start | bytes 3076
  66.8 4.7 %collective-permute-start = (bf16[3,896]{1,0:T(4,128)(2,1)S(1)}, bf16[3,896]{1,0:T(4,128)(2,1)S(1)}, u32[]{:S(2)}, u32[]{:S(2)}) collective-permute-start(bf16[3,896]{1,0:T(4,128)(2,1)S(1)} %pad_maximum_fusion.3), channel_id=1, source_target_pairs={{0,4},{4,8},{8,12},{12,16},{16,20},{20,24},{24,28},{1,5},{5,9},{9,... | collective-permute-start | bytes 16136 | tf_op jit(solution)/shard_map/ppermute | solution.py:12
  75.0 12.1 %copy-start.6 = (s32[259]{0:T(512)S(1)}, s32[259]{0:T(512)}, u32[]{:S(2)}) copy-start(s32[259]{0:T(512)} %copy-done.5) | copy-start | bytes 3112
  78.1 14.1 %collective-permute-start.2 = (f32[6,65,256]{2,1,0:T(8,128)}, f32[6,65,256]{2,1,0:T(8,128)}, u32[]{:S(2)}, u32[]{:S(2)}) collective-permute-start(f32[6,65,256]{2,1,0:T(8,128)} %pad_maximum_fusion), channel_id=1, source_target_pairs={{0,8},{4,12},{8,16},{12,20},{16,24},{20,28},{1,9},{5,13},{9,17},{1... | collective-permute-start | bytes 1198088 | tf_op jit(solution)/shard_map/ppermute | solution.py:12
  83.9 11.2 %collective-permute-start.1 = (f32[6,65,256]{2,1,0:T(8,128)}, f32[6,65,256]{2,1,0:T(8,128)}, u32[]{:S(2)}, u32[]{:S(2)}) collective-permute-start(f32[6,65,256]{2,1,0:T(8,128)} %pad_maximum_fusion), channel_id=1, source_target_pairs={{0,4},{4,8},{8,12},{12,16},{16,20},{20,24},{24,28},{1,5},{5,9},{9,... | collective-permute-start | bytes 1198088 | tf_op jit(solution)/shard_map/ppermute | solution.py:12
  87.8 20.9 %copy-start.3 = (bf16[2048,384]{1,0:T(8,128)(2,1)S(1)}, bf16[2048,384]{1,0:T(8,128)(2,1)}, u32[]{:S(2)}) copy-start(bf16[2048,384]{1,0:T(8,128)(2,1)} %param.24) | copy-start | bytes 4718596
  97.2 18.7 %collective-permute-start.3 = (f32[6,65,256]{2,1,0:T(8,128)S(1)}, f32[6,65,256]{2,1,0:T(8,128)S(1)}, u32[]{:S(2)}, u32[]{:S(2)}) collective-permute-start(f32[6,65,256]{2,1,0:T(8,128)S(1)} %pad_maximum_fusion.1), channel_id=1, source_target_pairs={{0,8},{4,12},{8,16},{12,20},{16,24},{20,28},{1,9},{5,13},{9,17},{1... | collective-permute-start | bytes 1198088 | tf_op jit(solution)/shard_map/ppermute | solution.py:12
  110.2 11.6 %copy-start.2 = (f32[256,384]{0,1:T(8,128)S(1)}, f32[256,384]{0,1:T(8,128)}, u32[]{:S(2)}) copy-start(f32[256,384]{0,1:T(8,128)} %copy.39) | copy-start | bytes 1179652
  110.2 11.6 %copy-start.8 = (f32[1,6,2,128]{3,1,2,0:T(8,128)S(1)}, f32[1,6,2,128]{3,1,2,0:T(8,128)}, u32[]{:S(2)}) copy-start(f32[1,6,2,128]{3,1,2,0:T(8,128)} %copy-done.7) | copy-start | bytes 18436
  115.9 12.2 %copy-start.20 = (f32[6]{0:T(128)S(1)}, f32[6]{0:T(128)}, u32[]{:S(2)}) copy-start(f32[6]{0:T(128)} %param.31) | copy-start | bytes 76
  116.0 12.2 %collective-permute-start.4 = (f32[6,65,256]{2,1,0:T(8,128)S(1)}, f32[6,65,256]{2,1,0:T(8,128)S(1)}, u32[]{:S(2)}, u32[]{:S(2)}) collective-permute-start(f32[6,65,256]{2,1,0:T(8,128)S(1)} %pad_maximum_fusion.2), channel_id=1, source_target_pairs={{0,16},{4,20},{8,24},{12,28},{1,17},{5,21},{9,25},{13,29},{2,18},{... | collective-permute-start | bytes 1198088 | tf_op jit(solution)/shard_map/ppermute | solution.py:12
  128.7 2.0 %copy-start.18 = (pred[8]{0:T(512)(128)(4,1)S(1)}, pred[8]{0:T(512)(128)(4,1)}, u32[]{:S(2)}) copy-start(pred[8]{0:T(512)(128)(4,1)} %get-tuple-element.59) | copy-start | bytes 28
Sparse Core Ops, SparseCore 0:
  24.4 15.7 all-gather.2
  41.8 22.5 all-gather.4
where the time goes:
time: 162 us; the launch traced here: 161 us
  waiting for transfers between devices  51.2 us (32%)
  starting transfers between devices  36.3 us (22%)
  blocking collectives  22.9 us (14%)
  other arithmetic  15.7 us (10%)
  between operations  14.4 us (9%)
  matrix products  11.6 us (7%)
  local copies, waits for them, and re-layouts  9.22 us (6%)
    ppermute x5, starting transfers between devices, shifted(): return lax.ppermute(array, axis, pairs)  28.8 us
    all_to_all x1, blocking collectives, per_device(): lax.all_to_all(outgoing, 'seq', split_axis=0, concat_axis=0, tiled=True)  22.9 us
    all_gather x1, waiting for transfers between devices, per_device(): w_full = lax.all_gather(shared_weight, 'fsdp', axis=0, tiled=True)  17.1 us
    ppermute x5, waiting for transfers between devices, shifted(): return lax.ppermute(array, axis, pairs)  15.9 us
    all_gather x1, waiting for transfers between devices, per_device(): feature_part = lax.all_gather(stream_block, 'fsdp', axis=1, tiled=True)  11.1 us
    all_to_all x1, starting transfers between devices, per_device(): lax.all_to_all(slot_rows, 'seq', split_axis=0, concat_axis=0, tiled=True)  7.42 us
    dot_general x4, matrix products, per_device(): jnp.dot(feature_part, weight, preferred_element_type=jnp.float32)  7.29 us
    all_to_all x1, waiting for transfers between devices, per_device(): lax.all_to_all(slot_rows, 'seq', split_axis=0, concat_axis=0, tiled=True)  6.42 us
  transfers between devices with their start and end apart: 8, of which 8 were waited for; matrix products, arithmetic and copies ran while one was open for 13% of the time, Pallas kernels for 0%

commit v1 on v0

--- a/solution.py
+++ b/solution.py
@@ -114,7 +114,12 @@
     state_dim = shared_weight.shape[1] // 2
     w_full = lax.all_gather(shared_weight, "fsdp", axis=0, tiled=True)
     weight_list = (x_weight, z_weight, step_weight, w_full)
-    feature_part = lax.all_gather(stream_block, "fsdp", axis=1, tiled=True)
+    ring = [stream_block]
+    for hop in range(3):
+        ring.append(lax.ppermute(ring[-1], "fsdp", [(dev, (dev + 1) % 4) for dev in range(4)]))
+    feature_part = jnp.roll(
+        jnp.concatenate(ring[::-1], axis=1), (lax.axis_index("fsdp") + 1) * ring[0].shape[1], axis=1
+    )
     x_acc, z_acc, step_acc, bc_acc = tuple(
         (
             jnp.dot(feature_part, weight, preferred_element_type=jnp.float32)

time: 162 us -> 149 us (0.920)
  blocking collectives: 22.9 us -> 33.2 us
  waiting for transfers between devices: 51.2 us -> 41.7 us
  other arithmetic: 15.7 us -> 9.43 us
  starting transfers between devices: 36.3 us -> 30.5 us
  local copies, waits for them, and re-layouts: 9.22 us -> 7.54 us
    ppermute x0 -> x3, waiting for transfers between devices: none -> 21.6 us  [per_device(): lax.ppermute(ring[-1], 'fsdp', [(dev, (dev + 1) % 4) for dev in range(4)])]
    all_gather x1, waiting for transfers between devices: 17.1 us -> 0.02 us  [per_device(): w_full = lax.all_gather(shared_weight, 'fsdp', axis=0, tiled=True)]
    all_gather x1 -> x0, waiting for transfers between devices: 11.1 us -> none  [per_device(): feature_part = lax.all_gather(stream_block, 'fsdp', axis=1, tiled=True)]
    all_to_all x1, blocking collectives: 22.9 us -> 33.2 us  [per_device(): lax.all_to_all(outgoing, 'seq', split_axis=0, concat_axis=0, tiled=True)]
    ppermute x5, starting transfers between devices: 28.8 us -> 21.9 us  [shifted(): return lax.ppermute(array, axis, pairs)]
    slice x2, local copies, waits for them, and re-layouts: 2.68 us -> 0.19 us  [per_device(): x_heads = activated[:, :inner_dev].reshape(tok_dev, heads_dev, head_dim)]
    ppermute x5, waiting for transfers between devices: 15.9 us -> 13.8 us  [shifted(): return lax.ppermute(array, axis, pairs)]
    unnamed x52 -> x31, local copies, waits for them, and re-layouts: 1.2 us -> 2.93 us
  transfers between devices with their start and end apart: 8 -> 10, of which waited for: 8 -> 9; matrix products, arithmetic and copies ran while one was open for 13% -> 11% of each run, Pallas kernels for 0% -> 0%
where the time goes in v1:
time: 149 us; the launch traced here: 148 us
  waiting for transfers between devices  41.7 us (28%)
  blocking collectives  33.2 us (22%)
  starting transfers between devices  30.5 us (20%)
  between operations  14.5 us (10%)
  matrix products  11.2 us (8%)
  other arithmetic  9.43 us (6%)
  local copies, waits for them, and re-layouts  7.54 us (5%)
    all_to_all x1, blocking collectives, per_device(): lax.all_to_all(outgoing, 'seq', split_axis=0, concat_axis=0, tiled=True)  33.2 us
    ppermute x5, starting transfers between devices, shifted(): return lax.ppermute(array, axis, pairs)  21.9 us
    ppermute x3, waiting for transfers between devices, per_device(): lax.ppermute(ring[-1], 'fsdp', [(dev, (dev + 1) % 4) for dev in range(4)])  21.6 us
    ppermute x5, waiting for transfers between devices, shifted(): return lax.ppermute(array, axis, pairs)  13.8 us
    all_to_all x1, starting transfers between devices, per_device(): lax.all_to_all(slot_rows, 'seq', split_axis=0, concat_axis=0, tiled=True)  7.42 us
    dot_general x4, matrix products, per_device(): jnp.dot(feature_part, weight, preferred_element_type=jnp.float32)  7.1 us
    all_to_all x1, waiting for transfers between devices, per_device(): lax.all_to_all(slot_rows, 'seq', split_axis=0, concat_axis=0, tiled=True)  5.63 us
  transfers between devices with their start and end apart: 10, of which 9 were waited for; matrix products, arithmetic and copies ran while one was open for 11% of the time, Pallas kernels for 0%

profile of v1, /device:TPU:0, one launch (start us, length us, event | category | flops | bytes accessed | tf_op | source)
XLA Modules:
  0.0 148.0 jit_solution(18145284165127408943)
XLA Ops:
  6.5 7.4 %all-to-all-start = ((bf16[8,32,512]{2,1,0:T(8,128)(2,1)}), bf16[8,32,512]{2,1,0:T(8,128)(2,1)S(1)}, u32[]{:S(2)}, u32[]{:S(2)}) async-start(bf16[8,32,512]{2,1,0:T(8,128)(2,1)} %bitcast.81), calls=%async_computation | async-start | bytes 524288 | tf_op jit(solution)/shard_map/all_to_all | solution.py:107
  14.0 0.0 all-gather.2.cloned.1.call-start
  14.0 0.7 all-gather.2.cloned.1.call-update
  14.7 0.7 compare_and_fusion.1
  15.4 1.0 sort.17
  16.4 0.1 broadcast_in_dim.93
  16.5 0.1 broadcast_in_dim.94
  16.6 0.7 constant_dynamic-update-slice_fusion.1
  17.3 5.6 %all-to-all-done = bf16[8,32,512]{2,1,0:T(8,128)(2,1)S(1)} async-done(((bf16[8,32,512]{2,1,0:T(8,128)(2,1)}), bf16[8,32,512]{2,1,0:T(8,128)(2,1)S(1)}, u32[]{:S(2)}, u32[]{:S(2)}) %all-to-all-start) | async-done | bytes 262176 | tf_op jit(solution)/shard_map/all_to_all | solution.py:107
  22.9 0.6 gather_fusion
  23.5 0.1 bitcast_select_fusion
  23.6 0.1 collective-permute-start
  23.6 0.2 reduce-window.18
  23.8 0.1 convert_reduce_fusion
  23.9 9.1 %collective-permute-done = bf16[256,512]{1,0:T(8,128)(2,1)S(1)} collective-permute-done((bf16[256,512]{1,0:T(8,128)(2,1)S(1)}, bf16[256,512]{1,0:T(8,128)(2,1)S(1)}, u32[]{:S(2)}, u32[]{:S(2)}) %collective-permute-start) | collective-permute-done | bytes 262176 | tf_op jit(solution)/shard_map/ppermute | solution.py:119
  33.0 1.0 collective-permute-start.1
  34.0 0.7 fusion.61
  35.4 0.7 broadcast_compare_fusion
  36.1 7.4 %collective-permute-done.1 = bf16[256,512]{1,0:T(8,128)(2,1)S(1)} collective-permute-done((bf16[256,512]{1,0:T(8,128)(2,1)S(1)}, bf16[256,512]{1,0:T(8,128)(2,1)S(1)}, u32[]{:S(2)}, u32[]{:S(2)}) %collective-permute-start.1) | collective-permute-done | bytes 262176 | tf_op jit(solution)/shard_map/ppermute | solution.py:119
  43.5 0.6 slice.199
  44.1 5.1 %collective-permute-done.2 = bf16[256,512]{1,0:T(8,128)(2,1)S(1)} collective-permute-done((bf16[256,512]{1,0:T(8,128)(2,1)S(1)}, bf16[256,512]{1,0:T(8,128)(2,1)S(1)}, u32[]{:S(2)}, u32[]{:S(2)}) %collective-permute-start.2) | collective-permute-done | bytes 262176 | tf_op jit(solution)/shard_map/ppermute | solution.py:119
  49.5 1.3 copy-done.1
  50.9 0.4 fusion.45
  51.3 1.8 %reduce-window.19 = f32[6,2,128]{2,1,0:T(2,128)S(1)} reduce-window(f32[6,2,128]{2,1,0:T(2,128)S(1)} %reshape.288, f32[]{:T(128)} %constant.176.clone.1), window={size=1x1x128 pad=0_0x0_0x127_0}, to_apply=%region_3.4 | reduce-window | flops 195072 | bytes 12292 | tf_op jit(solution)/shard_map/reduce-window.1
  53.1 0.1 slice.222
  53.2 0.1 copy.40
  53.3 0.1 copy.41
  53.4 0.1 add_bitcast_fusion
  53.5 0.2 slice_reduce_fusion
  53.7 0.1 select_exponential_fusion.1
  53.8 1.9 %convolution_convert_fusion.2 = bf16[256,384]{1,0:T(8,128)(2,1)S(1)} fusion(bf16[2048,384]{1,0:T(8,128)(2,1)S(1)} %copy-done, bf16[256,4096]{1,0:T(8,128)(2,1)} %copy-done.1, s32[]{:T(128)S(6)} %select_n.84), kind=kOutput, calls=%fused_computation.14 | convolution fusion | flops 402751488 | bytes 2818052 | tf_op jit(solution)/shard_map/dot_general | solution.py:125
  55.8 2.6 %convolution_convert_fusion = bf16[256,512]{1,0:T(8,128)(2,1)S(1)} fusion(bf16[2048,512]{1,0:T(8,128)(2,1)} %all-gather.2.cloned.1.call-done, bf16[256,4096]{1,0:T(8,128)(2,1)} %copy-done.1, s32[]{:T(128)S(6)} %select_n.84), kind=kOutput, calls=%fused_computation.8 | convolution fusion | flops 537001984 | bytes 3407876 | tf_op jit(solution)/shard_map/dot_general | solution.py:125
  58.4 3.3 %collective-permute-start.3 = (bf16[3,896]{1,0:T(4,128)(2,1)S(1)}, bf16[3,896]{1,0:T(4,128)(2,1)S(1)}, u32[]{:S(2)}, u32[]{:S(2)}) collective-permute-start(bf16[3,896]{1,0:T(4,128)(2,1)S(1)} %pad_maximum_fusion.3), channel_id=1, source_target_pairs={{0,4},{4,8},{8,12},{12,16},{16,20},{20,24},{24,28},{1,5},{5,9},{9,... | collective-permute-start | bytes 16136 | tf_op jit(solution)/shard_map/ppermute | solution.py:12
  61.7 0.7 broadcast_select_fusion.1
  62.4 0.7 collective-permute-done.3
  63.1 0.1 maximum_convert_fusion
  63.2 0.7 divide_multiply_fusion
  63.9 0.2 copy.39
  64.1 0.5 fusion.29
  64.6 0.1 broadcast_in_dim.104
  64.7 5.0 %collective-permute-start.4 = (f32[6,65,256]{2,1,0:T(8,128)S(1)}, f32[6,65,256]{2,1,0:T(8,128)}, u32[]{:S(2)}, u32[]{:S(2)}) collective-permute-start(f32[6,65,256]{2,1,0:T(8,128)S(1)} %pad_maximum_fusion), channel_id=1, source_target_pairs={{0,4},{4,8},{8,12},{12,16},{16,20},{20,24},{24,28},{1,5},{5,9},{9,... | collective-permute-start | bytes 1198088 | tf_op jit(solution)/shard_map/ppermute | solution.py:12
  69.6 2.4 %collective-permute-start.5 = (f32[6,65,256]{2,1,0:T(8,128)S(1)}, f32[6,65,256]{2,1,0:T(8,128)}, u32[]{:S(2)}, u32[]{:S(2)}) collective-permute-start(f32[6,65,256]{2,1,0:T(8,128)S(1)} %pad_maximum_fusion), channel_id=1, source_target_pairs={{0,8},{4,12},{8,16},{12,20},{16,24},{20,28},{1,9},{5,13},{9,17},{1... | collective-permute-start | bytes 1198088 | tf_op jit(solution)/shard_map/ppermute | solution.py:12
  72.1 0.1 slice.182
  72.1 0.1 fusion.35
  72.3 4.2 %collective-permute-done.4 = f32[6,65,256]{2,1,0:T(8,128)} collective-permute-done((f32[6,65,256]{2,1,0:T(8,128)S(1)}, f32[6,65,256]{2,1,0:T(8,128)}, u32[]{:S(2)}, u32[]{:S(2)}) %collective-permute-start.4) | collective-permute-done | bytes 399392 | tf_op jit(solution)/shard_map/ppermute | solution.py:12
  76.4 2.5 %collective-permute-done.5 = f32[6,65,256]{2,1,0:T(8,128)} collective-permute-done((f32[6,65,256]{2,1,0:T(8,128)S(1)}, f32[6,65,256]{2,1,0:T(8,128)}, u32[]{:S(2)}, u32[]{:S(2)}) %collective-permute-start.5) | collective-permute-done | bytes 399392 | tf_op jit(solution)/shard_map/ppermute | solution.py:12
  78.9 0.8 fusion.51
  79.7 1.2 slice_add_fusion
  81.0 6.5 %collective-permute-start.6 = (f32[6,65,256]{2,1,0:T(8,128)S(1)}, f32[6,65,256]{2,1,0:T(8,128)S(1)}, u32[]{:S(2)}, u32[]{:S(2)}) collective-permute-start(f32[6,65,256]{2,1,0:T(8,128)S(1)} %pad_maximum_fusion.1), channel_id=1, source_target_pairs={{0,8},{4,12},{8,16},{12,20},{16,24},{20,28},{1,9},{5,13},{9,17},{1... | collective-permute-start | bytes 1198088 | tf_op jit(solution)/shard_map/ppermute | solution.py:12
  87.5 0.7 fusion.53
  88.2 2.1 %fusion.10 = f32[256,384]{1,0:T(8,128)S(1)} fusion(bf16[2048,384]{1,0:T(8,128)(2,1)} %param.24, bf16[256,4096]{1,0:T(8,128)(2,1)S(1)} %copy-done.2, s32[]{:T(128)S(6)} %select_n.84), kind=kOutput, calls=%fused_computation.13 | convolution fusion | flops 402849792 | bytes 3014660 | tf_op jit(solution)/shard_map/dot_general | solution.py:125
  90.3 2.9 %collective-permute-done.6 = f32[6,65,256]{2,1,0:T(8,128)S(1)} collective-permute-done((f32[6,65,256]{2,1,0:T(8,128)S(1)}, f32[6,65,256]{2,1,0:T(8,128)S(1)}, u32[]{:S(2)}, u32[]{:S(2)}) %collective-permute-start.6) | collective-permute-done | bytes 399392 | tf_op jit(solution)/shard_map/ppermute | solution.py:12
  93.3 0.1 fusion.28
  93.4 4.7 %collective-permute-start.7 = (f32[6,65,256]{2,1,0:T(8,128)S(1)}, f32[6,65,256]{2,1,0:T(8,128)S(1)}, u32[]{:S(2)}, u32[]{:S(2)}) collective-permute-start(f32[6,65,256]{2,1,0:T(8,128)S(1)} %pad_maximum_fusion.2), channel_id=1, source_target_pairs={{0,16},{4,20},{8,24},{12,28},{1,17},{5,21},{9,25},{13,29},{2,18},{... | collective-permute-start | bytes 1198088 | tf_op jit(solution)/shard_map/ppermute | solution.py:12
  98.1 0.4 fusion.37
  98.5 1.9 %fusion.5 = f32[256,6,64]{0,2,1:T(8,128)S(1)} fusion(f32[6,256]{1,0:T(8,128)S(1)} %bitcast.86, f32[256,256]{1,0:T(8,128)S(1)} %fusion.37, pred[256,256]{1,0:T(8,128)(4,1)S(1)} %fusion.35, f32[256,6,64]{0,2,1:T(8,128)S(1)} %bitcast.76, f32[256,6]{0,1:T(8,128)S(1)} %get-tuple-element.76), kind=kOutput, calls=%fused_computation.7 | convolution fusion | flops 303267840 | bytes 1126400 | tf_op jit(solution)/shard_map/hts,shp->thp/dot_general | solution.py:75
  100.4 3.6 %collective-permute-done.7 = f32[6,65,256]{2,1,0:T(8,128)S(1)} collective-permute-done((f32[6,65,256]{2,1,0:T(8,128)S(1)}, f32[6,65,256]{2,1,0:T(8,128)S(1)}, u32[]{:S(2)}, u32[]{:S(2)}) %collective-permute-start.7) | collective-permute-done | bytes 399392 | tf_op jit(solution)/shard_map/ppermute | solution.py:12
  104.0 1.3 fusion.9
  105.3 1.2 copy.42
  106.5 0.1 multiply_convert_fusion
  106.6 0.6 gather_fusion.1
  107.2 0.1 broadcast_select_fusion
  107.3 33.2 %all_to_all.10 = bf16[8,32,384]{2,1,0:T(8,128)(2,1)S(1)} all-to-all(bf16[8,32,384]{2,1,0:T(8,128)(2,1)S(1)} %broadcast_select_fusion), channel_id=1, replica_groups=mesh['seq'=8,'fsdp'=4] {'seq'}, dimensions={0} | all-to-all | bytes 393216 | tf_op jit(solution)/shard_map/all_to_all | solution.py:164
  140.5 0.7 copy.70
  (49 shorter events, 0.5 us)
Async XLA Ops:
  6.5 47.2 %copy-start = (bf16[2048,384]{1,0:T(8,128)(2,1)S(1)}, bf16[2048,384]{1,0:T(8,128)(2,1)}, u32[]{:S(2)}) copy-start(bf16[2048,384]{1,0:T(8,128)(2,1)} %param.23) | copy-start | bytes 4718596
  6.5 17.1 %copy-start.7 = (s32[4]{0:T(128)S(1)}, s32[4]{0:T(128)}, u32[]{:S(2)}) copy-start(s32[4]{0:T(128)} %param.22) | copy-start | bytes 52
  6.5 17.3 %copy-start.4 = (f32[4,512]{1,0:T(4,128)S(1)}, f32[4,512]{1,0:T(4,128)}, u32[]{:S(2)}) copy-start(f32[4,512]{1,0:T(4,128)} %param.28) | copy-start | bytes 24580
  6.5 37.6 %copy-start.8 = (f32[6]{0:T(128)S(1)}, f32[6]{0:T(128)}, u32[]{:S(2)}) copy-start(f32[6]{0:T(128)} %param.30) | copy-start | bytes 76
  6.5 16.3 %all-to-all-start = ((bf16[8,32,512]{2,1,0:T(8,128)(2,1)}), bf16[8,32,512]{2,1,0:T(8,128)(2,1)S(1)}, u32[]{:S(2)}, u32[]{:S(2)}) async-start(bf16[8,32,512]{2,1,0:T(8,128)(2,1)} %bitcast.81), calls=%async_computation | async-start | bytes 524288 | tf_op jit(solution)/shard_map/all_to_all | solution.py:107
  14.0 41.8 %all-gather.2.cloned.1.call-start = ((), (), s32[]{:S(2)}) async-start(), calls=%async_computation.2 | async-start | bytes 2621440 | tf_op jit(solution)/shard_map/all_gather | solution.py:115
  23.6 9.4 %collective-permute-start = (bf16[256,512]{1,0:T(8,128)(2,1)S(1)}, bf16[256,512]{1,0:T(8,128)(2,1)S(1)}, u32[]{:S(2)}, u32[]{:S(2)}) collective-permute-start(bf16[256,512]{1,0:T(8,128)(2,1)S(1)} %bitcast_select_fusion), channel_id=1, source_target_pairs={{0,1},{1,2},{2,3},{3,0},{4,5},{5,6},{6,7},{7,4},{8,9},{9,10},{10,1... | collective-permute-start | bytes 786440 | tf_op jit(solution)/shard_map/ppermute | solution.py:119
  33.0 10.5 %collective-permute-start.1 = (bf16[256,512]{1,0:T(8,128)(2,1)S(1)}, bf16[256,512]{1,0:T(8,128)(2,1)S(1)}, u32[]{:S(2)}, u32[]{:S(2)}) collective-permute-start(bf16[256,512]{1,0:T(8,128)(2,1)S(1)} %collective-permute-done), channel_id=1, source_target_pairs={{0,1},{1,2},{2,3},{3,0},{4,5},{5,6},{6,7},{7,4},{8,9},{9,10},{10,1... | collective-permute-start | bytes 786440 | tf_op jit(solution)/shard_map/ppermute | solution.py:119
  43.5 5.8 %collective-permute-start.2 = (bf16[256,512]{1,0:T(8,128)(2,1)S(1)}, bf16[256,512]{1,0:T(8,128)(2,1)S(1)}, u32[]{:S(2)}, u32[]{:S(2)}) collective-permute-start(bf16[256,512]{1,0:T(8,128)(2,1)S(1)} %collective-permute-done.1), channel_id=1, source_target_pairs={{0,1},{1,2},{2,3},{3,0},{4,5},{5,6},{6,7},{7,4},{8,9},{9,10},{10,1... | collective-permute-start | bytes 786440 | tf_op jit(solution)/shard_map/ppermute | solution.py:119
  44.1 6.8 %copy-start.3 = (bf16[2048,6]{0,1:T(8,128)(2,1)S(1)}, bf16[2048,6]{0,1:T(8,128)(2,1)}, u32[]{:S(2)}) copy-start(bf16[2048,6]{0,1:T(8,128)(2,1)} %param.26) | copy-start | bytes 73732
  44.1 6.7 %copy-start.5 = (f32[6]{0:T(128)S(1)}, f32[6]{0:T(128)}, u32[]{:S(2)}) copy-start(f32[6]{0:T(128)} %param.29) | copy-start | bytes 76
  49.5 1.4 copy-start.1
  58.4 4.7 %collective-permute-start.3 = (bf16[3,896]{1,0:T(4,128)(2,1)S(1)}, bf16[3,896]{1,0:T(4,128)(2,1)S(1)}, u32[]{:S(2)}, u32[]{:S(2)}) collective-permute-start(bf16[3,896]{1,0:T(4,128)(2,1)S(1)} %pad_maximum_fusion.3), channel_id=1, source_target_pairs={{0,4},{4,8},{8,12},{12,16},{16,20},{20,24},{24,28},{1,5},{5,9},{9,... | collective-permute-start | bytes 16136 | tf_op jit(solution)/shard_map/ppermute | solution.py:12
  64.7 11.7 %collective-permute-start.4 = (f32[6,65,256]{2,1,0:T(8,128)S(1)}, f32[6,65,256]{2,1,0:T(8,128)}, u32[]{:S(2)}, u32[]{:S(2)}) collective-permute-start(f32[6,65,256]{2,1,0:T(8,128)S(1)} %pad_maximum_fusion), channel_id=1, source_target_pairs={{0,4},{4,8},{8,12},{12,16},{16,20},{20,24},{24,28},{1,5},{5,9},{9,... | collective-permute-start | bytes 1198088 | tf_op jit(solution)/shard_map/ppermute | solution.py:12
  69.6 9.3 %collective-permute-start.5 = (f32[6,65,256]{2,1,0:T(8,128)S(1)}, f32[6,65,256]{2,1,0:T(8,128)}, u32[]{:S(2)}, u32[]{:S(2)}) collective-permute-start(f32[6,65,256]{2,1,0:T(8,128)S(1)} %pad_maximum_fusion), channel_id=1, source_target_pairs={{0,8},{4,12},{8,16},{12,20},{16,24},{20,28},{1,9},{5,13},{9,17},{1... | collective-permute-start | bytes 1198088 | tf_op jit(solution)/shard_map/ppermute | solution.py:12
  72.1 16.1 %copy-start.2 = (bf16[256,4096]{1,0:T(8,128)(2,1)S(1)}, bf16[256,4096]{1,0:T(8,128)(2,1)}, u32[]{:S(2)}) copy-start(bf16[256,4096]{1,0:T(8,128)(2,1)} %copy-done.1) | copy-start | bytes 6291460
  81.0 12.3 %collective-permute-start.6 = (f32[6,65,256]{2,1,0:T(8,128)S(1)}, f32[6,65,256]{2,1,0:T(8,128)S(1)}, u32[]{:S(2)}, u32[]{:S(2)}) collective-permute-start(f32[6,65,256]{2,1,0:T(8,128)S(1)} %pad_maximum_fusion.1), channel_id=1, source_target_pairs={{0,8},{4,12},{8,16},{12,20},{16,24},{20,28},{1,9},{5,13},{9,17},{1... | collective-permute-start | bytes 1198088 | tf_op jit(solution)/shard_map/ppermute | solution.py:12
  93.3 10.7 %copy-start.6 = (f32[6]{0:T(128)S(1)}, f32[6]{0:T(128)}, u32[]{:S(2)}) copy-start(f32[6]{0:T(128)} %param.31) | copy-start | bytes 76
  93.4 10.6 %collective-permute-start.7 = (f32[6,65,256]{2,1,0:T(8,128)S(1)}, f32[6,65,256]{2,1,0:T(8,128)S(1)}, u32[]{:S(2)}, u32[]{:S(2)}) collective-permute-start(f32[6,65,256]{2,1,0:T(8,128)S(1)} %pad_maximum_fusion.2), channel_id=1, source_target_pairs={{0,16},{4,20},{8,24},{12,28},{1,17},{5,21},{9,25},{13,29},{2,18},{... | collective-permute-start | bytes 1198088 | tf_op jit(solution)/shard_map/ppermute | solution.py:12
Sparse Core Ops, SparseCore 0:
  16.4 28.1 all-gather.1
